TPU v7x, 32 devices: a whole 2x2x4 slice. The times are simulated.
32 devices in a mesh: blk: 8 (over y, x, core), head: 4 (over z).
Axes of the slice: x: 2, y: 2, z: 4, core: 2. Of those that a mesh axis runs over, the one named last changes fastest.
Arguments:
- query_matrix: bfloat16 [4096, 4096], P(('blk', 'head')), may hold values from -6 to 6
- key_matrix: bfloat16 [4096, 512], P(('blk', 'head')), may hold values from -6 to 6
- value_matrix: bfloat16 [4096, 512], P(('blk', 'head')), may hold values from -6 to 6
- output_cotangent: bfloat16 [4096, 4096], P(('blk', 'head')), may hold values from -6 to 6
- forward_output: bfloat16 [4096, 4096], P(('blk', 'head')), may hold values from -6 to 6
- doc_ids: int32 [4096], P(('blk', 'head')), may hold values from 0 to 31, never falling along the last dimension, each value on 1 to 2048 neighbouring positions
Outputs:
- query_grad: bfloat16 [4096, 4096], P(('blk', 'head'))
- key_gradient: bfloat16 [4096, 512], P(('blk', 'head'))
- value_gradient: bfloat16 [4096, 512], P(('blk', 'head'))
Inputs may be any that keep to these rules, and one draw needn't show every extreme that they name: `doc_ids`: document numbers never fall along the window; every document has 2048 tokens or fewer and one has exactly 2048.
All inputs are finite; a program needn't handle non-finite values.
Results may differ from a plain program's by a relative error of at most 0.0051.
Values may be sent and summed in bfloat16 or wider, within the bound.
No kernel may reach another device: no remote copies, remote signals or barrier semaphores. Data moves between devices by JAX's collectives and lax.ppermute only.
A program may use at most 64 MiB of HBM per device.

v0:
```python
import functools

import jax
import jax.numpy as jnp
from jax import lax
from jax.experimental import pallas as pl
from jax.experimental.pallas import tpu as pltpu
from jax.sharding import PartitionSpec as P

HEAD_WIDTH = 128
DOC_SPAN = 4


masked_score = -1e30


def shifted(block, axis, distance):
    devices = range(lax.axis_size(axis))
    route = [(i - distance, i) for i in devices if i - distance in devices]
    return lax.ppermute(block, axis, route)


def attn_kernel(flags_ref, q_ref, do_ref, rt_ref, qdoc_ref, kdoc_ref, k_ref, v_ref,
                dq_ref, dk_ref, dv_ref, m_ref, l_ref, *, n_near, logit_scale):
    head = pl.program_id(0)
    rows = q_ref.shape[0]

    @pl.when(head == 0)
    def _():
        dk_ref[...] = jnp.zeros_like(dk_ref)
        dv_ref[...] = jnp.zeros_like(dv_ref)

    q = q_ref[...]
    do = do_ref[...]
    qdoc = qdoc_ref[...]
    row_id = lax.broadcasted_iota(jnp.int32, (rows, rows), 0)
    col_id = lax.broadcasted_iota(jnp.int32, (rows, rows), 1)

    def allowed_of(d):
        same = qdoc == kdoc_ref[d]
        if d == 0:
            same = same & (col_id <= row_id)
        return same

    def scores_of(d):
        s = lax.dot_general(q, k_ref[d], (((1,), (1,)), ((), ())),
                            preferred_element_type=jnp.float32) * logit_scale
        return s

    m_ref[...] = jnp.full(m_ref.shape, masked_score, jnp.float32)
    l_ref[...] = jnp.zeros(l_ref.shape, jnp.float32)
    for d in range(n_near):
        @pl.when(flags_ref[d] > 0)
        def _():
            allowed = allowed_of(d)
            s = jnp.where(allowed, scores_of(d), masked_score)
            m_old = m_ref[...]
            m_new = jnp.maximum(m_old, jnp.max(s, axis=-1, keepdims=True))
            l_ref[...] = l_ref[...] * jnp.exp(m_old - m_new) + jnp.sum(
                jnp.where(allowed, jnp.exp(s - m_new), 0.0), axis=-1, keepdims=True)
            m_ref[...] = m_new

    log_total = m_ref[...] + jnp.log(l_ref[...])
    rt = rt_ref[0]
    dq_ref[...] = jnp.zeros_like(dq_ref)
    for d in range(n_near):
        @pl.when(flags_ref[d] > 0)
        def _():
            allowed = allowed_of(d)
            s = scores_of(d)
            p = jnp.where(allowed, jnp.exp(s - log_total), 0.0)
            dp = lax.dot_general(do, v_ref[d], (((1,), (1,)), ((), ())),
                                 preferred_element_type=jnp.float32)
            ds = (p * (dp - rt)).astype(jnp.bfloat16)
            pb = p.astype(jnp.bfloat16)
            dv_ref[d] += lax.dot_general(pb, do, (((0,), (0,)), ((), ())),
                                         preferred_element_type=jnp.float32)
            dk_ref[d] += lax.dot_general(ds, q, (((0,), (0,)), ((), ())),
                                         preferred_element_type=jnp.float32)
            dq_ref[...] += jnp.dot(ds, k_ref[d], preferred_element_type=jnp.float32)


def block_attention(flags, q, do, rt, qdoc, kdoc, k, v):
    rows, cols = q.shape
    heads = cols // HEAD_WIDTH
    n_near = k.shape[0]
    kern = functools.partial(attn_kernel, n_near=n_near, logit_scale=HEAD_WIDTH ** (-0.5))
    full3 = lambda shape: pl.BlockSpec(shape, lambda h, f: (0, 0, 0))
    flops = 2 * heads * n_near * rows * rows * HEAD_WIDTH * 6
    return pl.pallas_call(
        kern,
        out_shape=(
            jax.ShapeDtypeStruct((rows, cols), jnp.float32),
            jax.ShapeDtypeStruct((n_near, rows, HEAD_WIDTH), jnp.float32),
            jax.ShapeDtypeStruct((n_near, rows, HEAD_WIDTH), jnp.float32),
        ),
        grid_spec=pltpu.PrefetchScalarGridSpec(
            num_scalar_prefetch=1,
            grid=(heads,),
            in_specs=[
                pl.BlockSpec((rows, HEAD_WIDTH), lambda h, f: (0, h)),
                pl.BlockSpec((rows, HEAD_WIDTH), lambda h, f: (0, h)),
                pl.BlockSpec((1, rows, 1), lambda h, f: (h, 0, 0)),
                pl.BlockSpec((rows, 1), lambda h, f: (0, 0)),
                full3((n_near, 1, rows)),
                full3((n_near, rows, HEAD_WIDTH)),
                full3((n_near, rows, HEAD_WIDTH)),
            ],
            out_specs=[
                pl.BlockSpec((rows, HEAD_WIDTH), lambda h, f: (0, h)),
                full3((n_near, rows, HEAD_WIDTH)),
                full3((n_near, rows, HEAD_WIDTH)),
            ],
            scratch_shapes=[pltpu.VMEM((rows, 1), jnp.float32), pltpu.VMEM((rows, 1), jnp.float32)],
        ),
        compiler_params=pltpu.CompilerParams(dimension_semantics=("arbitrary",)),
        cost_estimate=pl.CostEstimate(flops=flops, transcendentals=2 * heads * n_near * rows * rows,
                                      bytes_accessed=4 * rows * cols * 2 + 8 * n_near * rows * HEAD_WIDTH * 2),
    )(flags, q, do, rt, qdoc, kdoc, k, v)


def per_device(query_matrix, key_matrix, value_matrix, output_cotangent, forward_output, doc_ids):
    cycle_size = lax.axis_size("blk")
    head_ways = lax.axis_size("head")
    shard_rows = query_matrix.shape[0]
    block_rows = shard_rows * head_ways
    query_heads = query_matrix.shape[1] // (HEAD_WIDTH * head_ways)
    kv_heads = key_matrix.shape[1] // (HEAD_WIDTH * head_ways)
    heads_per_group = query_heads // kv_heads
    q_cols = query_heads * HEAD_WIDTH
    kv_cols = kv_heads * HEAD_WIDTH
    logit_scale = HEAD_WIDTH ** (-0.5)
    all_heads = query_matrix.shape[1] // HEAD_WIDTH

    row_terms_local = jnp.sum(
        output_cotangent.astype(jnp.float32).reshape(shard_rows, all_heads, HEAD_WIDTH)
        * forward_output.astype(jnp.float32).reshape(shard_rows, all_heads, HEAD_WIDTH),
        axis=-1,
    ).reshape(shard_rows, head_ways, query_heads)
    doc_half = jnp.broadcast_to(
        doc_ids.astype(jnp.bfloat16)[:, None, None], (shard_rows, head_ways, HEAD_WIDTH)
    )
    packed = jnp.concatenate(
        [
            query_matrix.reshape(shard_rows, head_ways, q_cols),
            output_cotangent.reshape(shard_rows, head_ways, q_cols),
            key_matrix.reshape(shard_rows, head_ways, kv_cols),
            value_matrix.reshape(shard_rows, head_ways, kv_cols),
            doc_half,
        ],
        axis=2,
    )
    packed = lax.all_to_all(packed, "head", split_axis=1, concat_axis=0, tiled=True)
    packed = packed.reshape(block_rows, 2 * q_cols + 2 * kv_cols + HEAD_WIDTH)
    row_terms_blk = lax.all_to_all(
        row_terms_local, "head", split_axis=1, concat_axis=0, tiled=True
    ).reshape(block_rows, query_heads)

    kvd_local = packed[:, 2 * q_cols :]

    my_block = lax.axis_index("blk")
    query_segment = kvd_local[:, 2 * kv_cols].astype(jnp.float32)
    first_segment = query_segment[0]

    span = min(DOC_SPAN, cycle_size - 1)
    near_blocks = [kvd_local]
    for distance in range(1, span + 1):
        near_blocks.append(shifted(kvd_local, "blk", distance))
    flags = [jnp.int32(1)]
    for distance in range(1, span + 1):
        last_segment = near_blocks[distance][block_rows - 1, 2 * kv_cols].astype(jnp.float32)
        flags.append(((my_block - distance >= 0) & (last_segment == first_segment)).astype(jnp.int32))
    flags = jnp.stack(flags)
    near_keys = jnp.stack([kvd[:, :kv_cols] for kvd in near_blocks])
    near_values = jnp.stack([kvd[:, kv_cols : 2 * kv_cols] for kvd in near_blocks])
    near_docs = jnp.stack([kvd[:, 2 * kv_cols].astype(jnp.float32) for kvd in near_blocks])[:, None, :]
    query_total, key_parts, value_parts = block_attention(
        flags,
        packed[:, :q_cols],
        packed[:, q_cols : 2 * q_cols],
        row_terms_blk.transpose(1, 0)[:, :, None],
        query_segment[:, None],
        near_docs,
        near_keys,
        near_values,
    )
    kv_grad = jnp.concatenate([key_parts[0], value_parts[0]], axis=1)
    for distance in range(1, span + 1):
        kv_grad = kv_grad + shifted(
            jnp.concatenate([key_parts[distance], value_parts[distance]], axis=1), "blk", -distance
        )

    query_grad = (query_total * logit_scale).astype(jnp.bfloat16)
    key_gradient = (kv_grad[:, :kv_cols] * logit_scale).astype(jnp.bfloat16)
    value_gradient = kv_grad[:, kv_cols:].astype(jnp.bfloat16)
    out_packed = jnp.concatenate([query_grad, key_gradient, value_gradient], axis=1).reshape(
        head_ways, shard_rows, 1, q_cols + 2 * kv_cols
    )
    out_packed = lax.all_to_all(out_packed, "head", split_axis=0, concat_axis=2, tiled=True)
    out_packed = out_packed.reshape(shard_rows, head_ways, q_cols + 2 * kv_cols)
    return (
        out_packed[:, :, :q_cols].reshape(shard_rows, head_ways * q_cols),
        out_packed[:, :, q_cols : q_cols + kv_cols].reshape(shard_rows, head_ways * kv_cols),
        out_packed[:, :, q_cols + kv_cols :].reshape(shard_rows, head_ways * kv_cols),
    )


def solution(mesh):
    return jax.shard_map(
        per_device,
        mesh=mesh,
        in_specs=(
            P(("blk", "head"), None),
            P(("blk", "head"), None),
            P(("blk", "head"), None),
            P(("blk", "head"), None),
            P(("blk", "head"), None),
            P(("blk", "head")),
        ),
        out_specs=(P(("blk", "head"), None), P(("blk", "head"), None), P(("blk", "head"), None)),
        check_vma=False,
    )
```

profile of v0, /device:TPU:14, one launch (start us, length us, event | category | flops | bytes accessed | tf_op | source)
XLA Modules:
  0.0 265.9 jit_solution(10519557488338153831)
XLA Ops:
  0.6 0.0 copy-start
  0.6 1.8 multiply_bitcast_fusion
  2.5 0.0 copy-start.6
  2.5 0.4 copy.46
  2.9 0.6 reduce_sum.9
  3.5 0.0 copy-start.5
  3.5 0.7 copy.35
  4.2 5.3 %all-to-all-start.1 = ((f32[128,4,8]{0,2,1:T(8,128)}), f32[128,4,8]{0,2,1:T(8,128)S(1)}, u32[]{:S(2)}, u32[]{:S(2)}) async-start(f32[128,4,8]{0,2,1:T(8,128)} %bitcast.13), calls=%async_computation.1 | async-start | bytes 32768 | tf_op jit(solution)/shard_map/all_to_all | solution.py:155
  9.5 1.3 bitcast_dynamic-update-slice_fusion.1
  10.8 1.3 bitcast_dynamic-update-slice_fusion
  12.2 0.1 broadcast_dynamic-update-slice_fusion
  12.4 1.4 copy-done.1
  13.8 0.0 all-to-all-done.1
  13.8 5.1 %all-to-all-start = ((bf16[128,4,2432]{2,0,1:T(8,128)(2,1)}), bf16[128,4,2432]{2,0,1:T(8,128)(2,1)S(1)}, u32[]{:S(2)}, u32[]{:S(2)}) async-start(bf16[128,4,2432]{2,0,1:T(8,128)(2,1)} %copy-done.1), calls=%async_computation | async-start | bytes 4980736 | tf_op jit(solution)/shard_map/all_to_all | solution.py:153
  18.9 2.0 copy.36.rt_ref
  20.9 50.8 %all-to-all-done = bf16[128,4,2432]{2,0,1:T(8,128)(2,1)S(1)} async-done(((bf16[128,4,2432]{2,0,1:T(8,128)(2,1)}), bf16[128,4,2432]{2,0,1:T(8,128)(2,1)S(1)}, u32[]{:S(2)}, u32[]{:S(2)}) %all-to-all-start) | async-done | bytes 2490400 | tf_op jit(solution)/shard_map/all_to_all | solution.py:153
  71.7 1.3 collective-permute-start.3
  73.0 1.3 collective-permute-start.2
  74.3 1.9 collective-permute-start
  76.3 1.6 fusion.14
  77.9 0.7 slice_reduce_fusion.4
  78.6 1.5 collective-permute-start.1
  80.1 0.7 fusion.8
  80.8 0.5 slice.165
  81.3 4.3 %collective-permute-done.3 = bf16[512,384]{1,0:T(8,128)(2,1)S(1)} collective-permute-done((bf16[512,384]{1,0:T(8,128)(2,1)S(1)}, bf16[512,384]{1,0:T(8,128)(2,1)S(1)}, u32[]{:S(2)}, u32[]{:S(2)}) %collective-permute-start.3) | collective-permute-done | bytes 393248 | tf_op jit(solution)/shard_map/ppermute | solution.py:20
  85.7 0.1 slice_reduce_fusion
  85.8 0.5 slice.168
  87.6 0.0 collective-permute-done.2
  87.6 0.5 slice.167
  89.5 0.1 slice_reduce_fusion.1
  89.6 3.0 %collective-permute-done.1 = bf16[512,384]{1,0:T(8,128)(2,1)S(1)} collective-permute-done((bf16[512,384]{1,0:T(8,128)(2,1)S(1)}, bf16[512,384]{1,0:T(8,128)(2,1)S(1)}, u32[]{:S(2)}, u32[]{:S(2)}) %collective-permute-start.1) | collective-permute-done | bytes 393248 | tf_op jit(solution)/shard_map/ppermute | solution.py:20
  92.5 0.6 slice.166
  94.4 0.1 slice_reduce_fusion.2
  94.5 0.0 collective-permute-done
  94.6 0.7 copy-done.3
  95.3 0.5 slice.164
  95.8 0.0 copy-done.4
  97.1 0.1 stack.70
  97.2 0.5 stack.71.flags_ref
  97.8 1.0 slice_reduce_fusion.3
  98.8 0.6 reshape.132.kdoc_ref
  99.4 1.7 fusion.7
  101.1 1.7 fusion.6
  102.8 0.7 fusion.5
  103.5 0.7 fusion.4
  104.2 94.4 %shard_map.85 = (f32[512,1024]{1,0:T(8,128)}, f32[5,512,128]{2,1,0:T(8,128)}, f32[5,512,128]{2,1,0:T(8,128)}) custom-call(s32[5]{0:T(128)} %stack.71.flags_ref, bf16[512,1024]{1,0:T(8,128)(2,1)} %get-tuple-element.17.q_ref, bf16[512,1024]{1,0:T(8,128)(2,1)} %get-tuple-element.16.do_ref, f32[8,512,1]{2,1,0:T(8,128)} %copy.36.rt_ref, ...), custom_call_target="tpu_custom_call" | custom-call | flops 16106127360 | bytes 9437184 | tf_op jit(solution)/shard_map/pallas_call | solution.py:90
  198.7 1.9 slice_bitcast_fusion.8
  200.6 2.1 collective-permute-start.4
  202.7 1.3 collective-permute-start.5
  204.1 1.3 collective-permute-start.6
  205.5 1.3 collective-permute-start.7
  206.8 0.3 multiply_convert_fusion
  207.1 6.7 %collective-permute-done.4 = f32[512,256]{1,0:T(8,128)S(1)} collective-permute-done((f32[512,256]{1,0:T(8,128)S(1)}, f32[512,256]{1,0:T(8,128)S(1)}, u32[]{:S(2)}, u32[]{:S(2)}) %collective-permute-start.4) | collective-permute-done | bytes 524320 | tf_op jit(solution)/shard_map/ppermute | solution.py:20
  213.8 11.2 %collective-permute-done.5 = f32[512,256]{1,0:T(8,128)S(1)} collective-permute-done((f32[512,256]{1,0:T(8,128)S(1)}, f32[512,256]{1,0:T(8,128)S(1)}, u32[]{:S(2)}, u32[]{:S(2)}) %collective-permute-start.5) | collective-permute-done | bytes 524320 | tf_op jit(solution)/shard_map/ppermute | solution.py:20
  225.0 0.0 collective-permute-done.6
  225.0 0.0 collective-permute-done.7
  225.0 0.2 fusion.2
  225.2 0.1 pad_maximum_fusion
  225.4 36.8 %all_to_all.45 = bf16[4,128,1,1280]{3,1,2,0:T(8,128)(2,1)S(1)} all-to-all(bf16[4,128,1,1280]{3,1,2,0:T(8,128)(2,1)S(1)} %bitcast.121), channel_id=1, replica_groups=mesh['blk'=8,'head'=4] {'head'}, dimensions={0} | all-to-all | bytes 2621440 | tf_op jit(solution)/shard_map/all_to_all | solution.py:199
  262.2 0.8 copy.38
  263.0 0.1 slice.188
  263.1 1.3 copy.39
  264.4 0.8 copy.41
  265.1 0.8 copy.40
  (25 shorter events, 0.4 us)
Async XLA Ops:
  0.6 11.5 %copy-start = (bf16[128,512]{1,0:T(8,128)(2,1)S(1)}, bf16[128,512]{1,0:T(8,128)(2,1)}, u32[]{:S(2)}) copy-start(bf16[128,512]{1,0:T(8,128)(2,1)} %param.7) | copy-start | bytes 393220
  2.5 7.0 %copy-start.6 = (s32[128]{0:T(128)S(1)}, s32[128]{0:T(128)}, u32[]{:S(2)}) copy-start(s32[128]{0:T(128)} %param.11) | copy-start | bytes 1540
  3.5 8.7 %copy-start.5 = (bf16[128,512]{1,0:T(8,128)(2,1)S(1)}, bf16[128,512]{1,0:T(8,128)(2,1)}, u32[]{:S(2)}) copy-start(bf16[128,512]{1,0:T(8,128)(2,1)} %param.8) | copy-start | bytes 393220
  4.2 9.6 %all-to-all-start.1 = ((f32[128,4,8]{0,2,1:T(8,128)}), f32[128,4,8]{0,2,1:T(8,128)S(1)}, u32[]{:S(2)}, u32[]{:S(2)}) async-start(f32[128,4,8]{0,2,1:T(8,128)} %bitcast.13), calls=%async_computation.1 | async-start | bytes 32768 | tf_op jit(solution)/shard_map/all_to_all | solution.py:155
  12.4 1.4 copy-start.1
  13.8 57.9 %all-to-all-start = ((bf16[128,4,2432]{2,0,1:T(8,128)(2,1)}), bf16[128,4,2432]{2,0,1:T(8,128)(2,1)S(1)}, u32[]{:S(2)}, u32[]{:S(2)}) async-start(bf16[128,4,2432]{2,0,1:T(8,128)(2,1)} %copy-done.1), calls=%async_computation | async-start | bytes 4980736 | tf_op jit(solution)/shard_map/all_to_all | solution.py:153
  71.7 13.9 %collective-permute-start.3 = (bf16[512,384]{1,0:T(8,128)(2,1)S(1)}, bf16[512,384]{1,0:T(8,128)(2,1)S(1)}, u32[]{:S(2)}, u32[]{:S(2)}) collective-permute-start(bf16[512,384]{1,0:T(8,128)(2,1)S(1)} %slice.163), channel_id=1, source_target_pairs={{0,16},{4,20},{8,24},{12,28},{1,17},{5,21},{9,25},{13,29},{2,18},{... | collective-permute-start | bytes 1179656 | tf_op jit(solution)/shard_map/ppermute | solution.py:20
  73.0 14.6 %collective-permute-start.2 = (bf16[512,384]{1,0:T(8,128)(2,1)S(1)}, bf16[512,384]{1,0:T(8,128)(2,1)S(1)}, u32[]{:S(2)}, u32[]{:S(2)}) collective-permute-start(bf16[512,384]{1,0:T(8,128)(2,1)S(1)} %slice.163), channel_id=1, source_target_pairs={{0,12},{4,16},{8,20},{12,24},{16,28},{1,13},{5,17},{9,21},{13,25},... | collective-permute-start | bytes 1179656 | tf_op jit(solution)/shard_map/ppermute | solution.py:20
  74.3 20.2 %collective-permute-start = (bf16[512,384]{1,0:T(8,128)(2,1)S(1)}, bf16[512,384]{1,0:T(8,128)(2,1)S(1)}, u32[]{:S(2)}, u32[]{:S(2)}) collective-permute-start(bf16[512,384]{1,0:T(8,128)(2,1)S(1)} %slice.163), channel_id=1, source_target_pairs={{0,4},{4,8},{8,12},{12,16},{16,20},{20,24},{24,28},{1,5},{5,9},{9,... | collective-permute-start | bytes 1179656 | tf_op jit(solution)/shard_map/ppermute | solution.py:20
  78.6 13.9 %collective-permute-start.1 = (bf16[512,384]{1,0:T(8,128)(2,1)S(1)}, bf16[512,384]{1,0:T(8,128)(2,1)S(1)}, u32[]{:S(2)}, u32[]{:S(2)}) collective-permute-start(bf16[512,384]{1,0:T(8,128)(2,1)S(1)} %slice.163), channel_id=1, source_target_pairs={{0,8},{4,12},{8,16},{12,20},{16,24},{20,28},{1,9},{5,13},{9,17},{1... | collective-permute-start | bytes 1179656 | tf_op jit(solution)/shard_map/ppermute | solution.py:20
  92.5 3.3 %copy-start.4 = (bf16[512,384]{1,0:T(8,128)(2,1)}, bf16[512,384]{1,0:T(8,128)(2,1)S(1)}, u32[]{:S(2)}) copy-start(bf16[512,384]{1,0:T(8,128)(2,1)S(1)} %collective-permute-done.1) | copy-start | bytes 1179652
  94.5 0.8 copy-start.3
  200.6 6.2 %copy-start.2 = (f32[512,1024]{1,0:T(8,128)S(1)}, f32[512,1024]{1,0:T(8,128)}, u32[]{:S(2)}) copy-start(f32[512,1024]{1,0:T(8,128)} %get-tuple-element.6) | copy-start | bytes 6291460
  200.6 13.1 %collective-permute-start.4 = (f32[512,256]{1,0:T(8,128)S(1)}, f32[512,256]{1,0:T(8,128)S(1)}, u32[]{:S(2)}, u32[]{:S(2)}) collective-permute-start(f32[512,256]{1,0:T(8,128)S(1)} %pad_maximum_fusion.1), channel_id=1, source_target_pairs={{4,0},{8,4},{12,8},{16,12},{20,16},{24,20},{28,24},{5,1},{9,5},{13... | collective-permute-start | bytes 1572872 | tf_op jit(solution)/shard_map/ppermute | solution.py:20
  202.7 22.3 %collective-permute-start.5 = (f32[512,256]{1,0:T(8,128)S(1)}, f32[512,256]{1,0:T(8,128)S(1)}, u32[]{:S(2)}, u32[]{:S(2)}) collective-permute-start(f32[512,256]{1,0:T(8,128)S(1)} %pad_maximum_fusion.2), channel_id=1, source_target_pairs={{8,0},{12,4},{16,8},{20,12},{24,16},{28,20},{9,1},{13,5},{17,9},{2... | collective-permute-start | bytes 1572872 | tf_op jit(solution)/shard_map/ppermute | solution.py:20
  204.1 20.9 %collective-permute-start.6 = (f32[512,256]{1,0:T(8,128)S(1)}, f32[512,256]{1,0:T(8,128)S(1)}, u32[]{:S(2)}, u32[]{:S(2)}) collective-permute-start(f32[512,256]{1,0:T(8,128)S(1)} %pad_maximum_fusion.3), channel_id=1, source_target_pairs={{12,0},{16,4},{20,8},{24,12},{28,16},{13,1},{17,5},{21,9},{25,13},... | collective-permute-start | bytes 1572872 | tf_op jit(solution)/shard_map/ppermute | solution.py:20
  205.5 19.5 %collective-permute-start.7 = (f32[512,256]{1,0:T(8,128)S(1)}, f32[512,256]{1,0:T(8,128)S(1)}, u32[]{:S(2)}, u32[]{:S(2)}) collective-permute-start(f32[512,256]{1,0:T(8,128)S(1)} %pad_maximum_fusion.4), channel_id=1, source_target_pairs={{16,0},{20,4},{24,8},{28,12},{17,1},{21,5},{25,9},{29,13},{18,2},{... | collective-permute-start | bytes 1572872 | tf_op jit(solution)/shard_map/ppermute | solution.py:20
where the time goes:
time: 261 us; the launch traced here: 266 us
  Pallas kernels  94.4 us (36%)
  waiting for transfers between devices  76.1 us (29%)
  blocking collectives  36.8 us (14%)
  local copies, waits for them, and re-layouts  25.6 us (10%)
  starting transfers between devices  22.4 us (9%)
  between operations  6.22 us (2%)
  other arithmetic  4.41 us (2%)
    pallas_call x1, Pallas kernels, block_attention(): pl.pallas_call(kern, out_shape=(jax.ShapeDtypeStruct((rows, cols), jnp.fl...  94.4 us
    all_to_all x1, waiting for transfers between devices, per_device(): lax.all_to_all(packed, 'head', split_axis=1, concat_axis=0, tiled=True)  50.8 us
    all_to_all x1, blocking collectives, per_device(): lax.all_to_all(out_packed, 'head', split_axis=0, concat_axis=2, tiled=True)  36.8 us
    ppermute x8, waiting for transfers between devices, shifted(): return lax.ppermute(block, axis, route)  25.2 us
    unnamed x26, local copies, waits for them, and re-layouts  12.9 us
    ppermute x8, starting transfers between devices, shifted(): return lax.ppermute(block, axis, route)  12 us
    all_to_all x1, starting transfers between devices, per_device(): lax.all_to_all(row_terms_local, 'head', split_axis=1, concat_axis=0, tile...  5.32 us
  transfers between devices with their start and end apart: 10, of which 5 were waited for; matrix products, arithmetic and copies ran while one was open for 4% of the time, Pallas kernels for 0%

commit v1 on v0

--- a/solution.py
+++ b/solution.py
@@ -140,23 +140,28 @@
     doc_half = jnp.broadcast_to(
         doc_ids.astype(jnp.bfloat16)[:, None, None], (shard_rows, head_ways, HEAD_WIDTH)
     )
-    packed = jnp.concatenate(
+    kvd_local = jnp.concatenate(
         [
-            query_matrix.reshape(shard_rows, head_ways, q_cols),
-            output_cotangent.reshape(shard_rows, head_ways, q_cols),
             key_matrix.reshape(shard_rows, head_ways, kv_cols),
             value_matrix.reshape(shard_rows, head_ways, kv_cols),
             doc_half,
         ],
         axis=2,
     )
-    packed = lax.all_to_all(packed, "head", split_axis=1, concat_axis=0, tiled=True)
-    packed = packed.reshape(block_rows, 2 * q_cols + 2 * kv_cols + HEAD_WIDTH)
+    kvd_local = lax.all_to_all(kvd_local, "head", split_axis=1, concat_axis=0, tiled=True)
+    kvd_local = kvd_local.reshape(block_rows, 2 * kv_cols + HEAD_WIDTH)
     row_terms_blk = lax.all_to_all(
         row_terms_local, "head", split_axis=1, concat_axis=0, tiled=True
     ).reshape(block_rows, query_heads)
-
-    kvd_local = packed[:, 2 * q_cols :]
+    packed = jnp.concatenate(
+        [
+            query_matrix.reshape(shard_rows, head_ways, q_cols),
+            output_cotangent.reshape(shard_rows, head_ways, q_cols),
+        ],
+        axis=2,
+    )
+    packed = lax.all_to_all(packed, "head", split_axis=1, concat_axis=0, tiled=True)
+    packed = packed.reshape(block_rows, 2 * q_cols)
 
     my_block = lax.axis_index("blk")
     query_segment = kvd_local[:, 2 * kv_cols].astype(jnp.float32)
@@ -184,24 +189,27 @@
         near_keys,
         near_values,
     )
+    query_grad = (query_total * logit_scale).astype(jnp.bfloat16).reshape(
+        head_ways, shard_rows, 1, q_cols
+    )
+    query_grad = lax.all_to_all(query_grad, "head", split_axis=0, concat_axis=2, tiled=True)
     kv_grad = jnp.concatenate([key_parts[0], value_parts[0]], axis=1)
     for distance in range(1, span + 1):
-        kv_grad = kv_grad + shifted(
-            jnp.concatenate([key_parts[distance], value_parts[distance]], axis=1), "blk", -distance
+        sent = jnp.concatenate([key_parts[distance], value_parts[distance]], axis=1)
+        kv_grad = kv_grad + shifted(sent.astype(jnp.bfloat16), "blk", -distance).astype(
+            jnp.float32
         )
-
-    query_grad = (query_total * logit_scale).astype(jnp.bfloat16)
     key_gradient = (kv_grad[:, :kv_cols] * logit_scale).astype(jnp.bfloat16)
     value_gradient = kv_grad[:, kv_cols:].astype(jnp.bfloat16)
-    out_packed = jnp.concatenate([query_grad, key_gradient, value_gradient], axis=1).reshape(
-        head_ways, shard_rows, 1, q_cols + 2 * kv_cols
+    out_packed = jnp.concatenate([key_gradient, value_gradient], axis=1).reshape(
+        head_ways, shard_rows, 1, 2 * kv_cols
     )
     out_packed = lax.all_to_all(out_packed, "head", split_axis=0, concat_axis=2, tiled=True)
-    out_packed = out_packed.reshape(shard_rows, head_ways, q_cols + 2 * kv_cols)
+    out_packed = out_packed.reshape(shard_rows, head_ways, 2 * kv_cols)
     return (
-        out_packed[:, :, :q_cols].reshape(shard_rows, head_ways * q_cols),
-        out_packed[:, :, q_cols : q_cols + kv_cols].reshape(shard_rows, head_ways * kv_cols),
-        out_packed[:, :, q_cols + kv_cols :].reshape(shard_rows, head_ways * kv_cols),
+        query_grad.reshape(shard_rows, head_ways * q_cols),
+        out_packed[:, :, :kv_cols].reshape(shard_rows, head_ways * kv_cols),
+        out_packed[:, :, kv_cols:].reshape(shard_rows, head_ways * kv_cols),
     )
 
 

time: 261 us -> 229 us (0.88); the launches traced: 266 us -> 226 us
  blocking collectives: 36.8 us -> 0 us
  starting transfers between devices: 22.4 us -> 43 us
  Pallas kernels: 94.4 us -> 76.7 us
  waiting for transfers between devices: 76.1 us -> 67.7 us
  other arithmetic: 4.41 us -> 10.8 us
  local copies, waits for them, and re-layouts: 25.6 us -> 21.6 us
    all_to_all x1, waiting for transfers between devices: 50.8 us -> 8.53 us  [per_device(): lax.all_to_all(packed, 'head', split_axis=1, concat_axis=0, tiled=True)]
    all_to_all x1 -> x0, blocking collectives: 36.8 us -> none  [per_device(): lax.all_to_all(out_packed, 'head', split_axis=0, concat_axis=2, tiled=True)]
    all_to_all x0 -> x3, waiting for transfers between devices: none -> 34.9 us  [the longest x1 21.3 us: per_device(): lax.all_to_all(query_grad, 'head', split_axis=0, concat_axis=2, tiled=True)]
    all_to_all x0 -> x3, starting transfers between devices: none -> 19.8 us  [the longest x1 9.07 us: per_device(): lax.all_to_all(out_packed, 'head', split_axis=0, concat_axis=2, tiled=True)]
    pallas_call x1, Pallas kernels: 94.4 us -> 76.7 us  [block_attention(): pl.pallas_call(kern, out_shape=(jax.ShapeDtypeStruct((rows, cols), jnp.fl...]
    ppermute x8, waiting for transfers between devices: 25.2 us -> 21 us  [shifted(): return lax.ppermute(block, axis, route)]
    unnamed x26 -> x24, local copies, waits for them, and re-layouts: 12.9 us -> 9.01 us
    all_to_all x1, waiting for transfers between devices: 0.01 us -> 3.27 us  [per_device(): lax.all_to_all(row_terms_local, 'head', split_axis=1, concat_axis=0, tile...]
  transfers between devices with their start and end apart: 10 -> 13, of which waited for: 5 -> 9; matrix products, arithmetic and copies ran while one was open for 4% -> 10% of each run, Pallas kernels for 0% -> 0%
where the time goes in v1:
time: 229 us; the launch traced here: 226 us
  Pallas kernels  76.7 us (33%)
  waiting for transfers between devices  67.7 us (30%)
  starting transfers between devices  43 us (19%)
  local copies, waits for them, and re-layouts  21.6 us (9%)
  other arithmetic  10.8 us (5%)
  between operations  6.2 us (3%)
    pallas_call x1, Pallas kernels, block_attention(): pl.pallas_call(kern, out_shape=(jax.ShapeDtypeStruct((rows, cols), jnp.fl...  76.7 us
    all_to_all x1, waiting for transfers between devices, per_device(): lax.all_to_all(query_grad, 'head', split_axis=0, concat_axis=2, tiled=True)  21.3 us
    ppermute x8, waiting for transfers between devices, shifted(): return lax.ppermute(block, axis, route)  21 us
    ppermute x8, starting transfers between devices, shifted(): return lax.ppermute(block, axis, route)  11.8 us
    all_to_all x1, starting transfers between devices, per_device(): lax.all_to_all(out_packed, 'head', split_axis=0, concat_axis=2, tiled=True)  9.07 us
    unnamed x24, local copies, waits for them, and re-layouts  9.01 us
    all_to_all x1, waiting for transfers between devices, per_device(): lax.all_to_all(packed, 'head', split_axis=1, concat_axis=0, tiled=True)  8.53 us
    all_to_all x1, waiting for transfers between devices, per_device(): lax.all_to_all(out_packed, 'head', split_axis=0, concat_axis=2, tiled=True)  7.16 us
  transfers between devices with their start and end apart: 13, of which 9 were waited for; matrix products, arithmetic and copies ran while one was open for 10% of the time, Pallas kernels for 0%

profile of v1, /device:TPU:14, one launch (start us, length us, event | category | flops | bytes accessed | tf_op | source)
XLA Modules:
  0.0 225.8 jit_solution(2559592895966785984)
XLA Ops:
  0.6 1.8 multiply_bitcast_fusion
  2.5 0.4 copy.49
  2.9 0.6 reduce_sum.9
  3.5 0.7 copy.36
  4.2 5.3 %all-to-all-start.2 = ((f32[128,4,8]{0,2,1:T(8,128)}), f32[128,4,8]{0,2,1:T(8,128)S(1)}, u32[]{:S(2)}, u32[]{:S(2)}) async-start(f32[128,4,8]{0,2,1:T(8,128)} %bitcast.18), calls=%async_computation.2 | async-start | bytes 32768 | tf_op jit(solution)/shard_map/all_to_all | solution.py:153
  9.6 0.1 broadcast_in_dim.15
  9.7 0.8 pad_maximum_fusion.1
  10.5 3.3 %all-to-all-done.2 = f32[128,4,8]{0,2,1:T(8,128)S(1)} async-done(((f32[128,4,8]{0,2,1:T(8,128)}), f32[128,4,8]{0,2,1:T(8,128)S(1)}, u32[]{:S(2)}, u32[]{:S(2)}) %all-to-all-start.2) | async-done | bytes 16416 | tf_op jit(solution)/shard_map/all_to_all | solution.py:153
  13.8 5.4 %all-to-all-start = ((bf16[128,4,384]{2,0,1:T(8,128)(2,1)}), bf16[128,4,384]{2,0,1:T(8,128)(2,1)}, u32[]{:S(2)}, u32[]{:S(2)}) async-start(bf16[128,4,384]{2,0,1:T(8,128)(2,1)} %pad_maximum_fusion.1), calls=%async_computation | async-start | bytes 786432 | tf_op jit(solution)/shard_map/all_to_all | solution.py:151
  19.2 0.2 copy_bitcast_fusion
  19.4 1.5 pad_maximum_fusion
  20.9 6.4 %all-to-all-done = bf16[128,4,384]{2,0,1:T(8,128)(2,1)} async-done(((bf16[128,4,384]{2,0,1:T(8,128)(2,1)}), bf16[128,4,384]{2,0,1:T(8,128)(2,1)}, u32[]{:S(2)}, u32[]{:S(2)}) %all-to-all-start) | async-done | bytes 393248 | tf_op jit(solution)/shard_map/all_to_all | solution.py:151
  27.4 6.1 %all-to-all-start.1 = ((bf16[128,4,2048]{2,0,1:T(8,128)(2,1)}), bf16[128,4,2048]{2,0,1:T(8,128)(2,1)S(1)}, u32[]{:S(2)}, u32[]{:S(2)}) async-start(bf16[128,4,2048]{2,0,1:T(8,128)(2,1)} %pad_maximum_fusion), calls=%async_computation.1 | async-start | bytes 4194304 | tf_op jit(solution)/shard_map/all_to_all | solution.py:163
  33.4 2.0 copy.37.rt_ref
  35.4 1.3 collective-permute-start.3
  36.7 1.3 collective-permute-start.2
  38.0 1.6 slice_reduce_fusion.4
  39.6 1.3 collective-permute-start.1
  40.9 2.1 collective-permute-start
  43.0 1.7 fusion.8
  44.7 1.2 slice.161
  45.9 3.6 %collective-permute-done.3 = bf16[512,384]{1,0:T(8,128)(2,1)S(1)} collective-permute-done((bf16[512,384]{1,0:T(8,128)(2,1)}, bf16[512,384]{1,0:T(8,128)(2,1)S(1)}, u32[]{:S(2)}, u32[]{:S(2)}) %collective-permute-start.3) | collective-permute-done | bytes 393248 | tf_op jit(solution)/shard_map/ppermute | solution.py:20
  49.5 0.1 slice_reduce_fusion
  49.7 0.5 slice.164
  51.5 0.5 slice.163
  53.3 0.1 slice_reduce_fusion.1
  53.5 3.6 %collective-permute-done.1 = bf16[512,384]{1,0:T(8,128)(2,1)S(1)} collective-permute-done((bf16[512,384]{1,0:T(8,128)(2,1)}, bf16[512,384]{1,0:T(8,128)(2,1)S(1)}, u32[]{:S(2)}, u32[]{:S(2)}) %collective-permute-start.1) | collective-permute-done | bytes 393248 | tf_op jit(solution)/shard_map/ppermute | solution.py:20
  57.1 0.5 slice.162
  58.9 0.1 slice_reduce_fusion.2
  59.1 0.7 copy-done.5
  59.8 0.5 slice.160
  61.6 0.1 stack.70
  61.7 0.5 stack.71.flags_ref
  62.3 1.0 slice_reduce_fusion.3
  63.3 0.6 reshape.142.kdoc_ref
  63.9 1.7 fusion.7
  65.6 0.7 fusion.6
  66.4 0.7 fusion.5
  67.1 0.7 fusion.4
  67.8 8.5 %all-to-all-done.1 = bf16[128,4,2048]{2,0,1:T(8,128)(2,1)S(1)} async-done(((bf16[128,4,2048]{2,0,1:T(8,128)(2,1)}), bf16[128,4,2048]{2,0,1:T(8,128)(2,1)S(1)}, u32[]{:S(2)}, u32[]{:S(2)}) %all-to-all-start.1) | async-done | bytes 2097184 | tf_op jit(solution)/shard_map/all_to_all | solution.py:163
  76.3 1.5 fusion.14
  77.9 76.7 %shard_map.85 = (f32[512,1024]{1,0:T(8,128)}, f32[5,512,128]{2,1,0:T(8,128)}, f32[5,512,128]{2,1,0:T(8,128)}) custom-call(s32[5]{0:T(128)} %stack.71.flags_ref, bf16[512,1024]{1,0:T(8,128)(2,1)} %get-tuple-element.13.q_ref, bf16[512,1024]{1,0:T(8,128)(2,1)} %get-tuple-element.12.do_ref, f32[8,512,1]{2,1,0:T(8,128)} %copy.37.rt_ref, ...), custom_call_target="tpu_custom_call" | custom-call | flops 16106127360 | bytes 9437184 | tf_op jit(solution)/shard_map/pallas_call | solution.py:90
  154.5 1.5 convert.45
  156.1 0.2 copy-done.3
  156.3 0.1 convert.46
  156.4 1.3 collective-permute-start.5
  157.8 1.3 collective-permute-start.6
  159.1 1.3 collective-permute-start.7
  160.5 1.9 collective-permute-start.4
  162.4 1.0 slice_bitcast_fusion.1
  163.4 2.3 %collective-permute-done.7 = bf16[512,256]{1,0:T(8,128)(2,1)S(1)} collective-permute-done((bf16[512,256]{1,0:T(8,128)(2,1)S(1)}, bf16[512,256]{1,0:T(8,128)(2,1)S(1)}, u32[]{:S(2)}, u32[]{:S(2)}) %collective-permute-start.7) | collective-permute-done | bytes 262176 | tf_op jit(solution)/shard_map/ppermute | solution.py:20
  165.8 11.4 %collective-permute-done.4 = bf16[512,256]{1,0:T(8,128)(2,1)S(1)} collective-permute-done((bf16[512,256]{1,0:T(8,128)(2,1)S(1)}, bf16[512,256]{1,0:T(8,128)(2,1)S(1)}, u32[]{:S(2)}, u32[]{:S(2)}) %collective-permute-start.4) | collective-permute-done | bytes 262176 | tf_op jit(solution)/shard_map/ppermute | solution.py:20
  177.1 0.1 fusion.2
  177.3 0.7 pad_maximum_fusion.6
  178.1 9.1 %all-to-all-start.4 = ((bf16[4,128,1,256]{3,1,2,0:T(8,128)(2,1)}), bf16[4,128,1,256]{3,1,2,0:T(8,128)(2,1)S(1)}, u32[]{:S(2)}, u32[]{:S(2)}) async-start(bf16[4,128,1,256]{3,1,2,0:T(8,128)(2,1)} %bitcast.50), calls=%async_computation.4 | async-start | bytes 524288 | tf_op jit(solution)/shard_map/all_to_all | solution.py:207
  187.1 1.2 multiply_convert_fusion
  188.4 7.2 %all-to-all-done.4 = bf16[4,128,1,256]{3,1,2,0:T(8,128)(2,1)S(1)} async-done(((bf16[4,128,1,256]{3,1,2,0:T(8,128)(2,1)}), bf16[4,128,1,256]{3,1,2,0:T(8,128)(2,1)S(1)}, u32[]{:S(2)}, u32[]{:S(2)}) %all-to-all-start.4) | async-done | bytes 262176 | tf_op jit(solution)/shard_map/all_to_all | solution.py:207
  195.5 5.3 %all-to-all-start.3 = ((bf16[4,128,1,1024]{3,1,2,0:T(8,128)(2,1)}), bf16[4,128,1,1024]{3,1,2,0:T(8,128)(2,1)S(1)}, u32[]{:S(2)}, u32[]{:S(2)}) async-start(bf16[4,128,1,1024]{3,1,2,0:T(8,128)(2,1)} %bitcast.35), calls=%async_computation.3 | async-start | bytes 2097152 | tf_op jit(solution)/shard_map/all_to_all | solution.py:195
  200.8 0.2 copy.41
  201.0 0.8 copy.44
  201.8 0.8 copy.43
  202.6 21.3 %all-to-all-done.3 = bf16[4,128,1,1024]{3,1,2,0:T(8,128)(2,1)S(1)} async-done(((bf16[4,128,1,1024]{3,1,2,0:T(8,128)(2,1)}), bf16[4,128,1,1024]{3,1,2,0:T(8,128)(2,1)S(1)}, u32[]{:S(2)}, u32[]{:S(2)}) %all-to-all-start.3) | async-done | bytes 1048608 | tf_op jit(solution)/shard_map/all_to_all | solution.py:195
  223.9 0.7 copy.39
  224.5 1.3 copy.42
  (36 shorter events, 0.5 us)
Async XLA Ops:
  0.6 8.9 %copy-start = (bf16[128,512]{1,0:T(8,128)(2,1)S(1)}, bf16[128,512]{1,0:T(8,128)(2,1)}, u32[]{:S(2)}) copy-start(bf16[128,512]{1,0:T(8,128)(2,1)} %param.7) | copy-start | bytes 393220
  2.9 6.7 %copy-start.7 = (s32[128]{0:T(128)S(1)}, s32[128]{0:T(128)}, u32[]{:S(2)}) copy-start(s32[128]{0:T(128)} %param.11) | copy-start | bytes 1540
  2.9 6.7 %copy-start.6 = (bf16[128,512]{1,0:T(8,128)(2,1)S(1)}, bf16[128,512]{1,0:T(8,128)(2,1)}, u32[]{:S(2)}) copy-start(bf16[128,512]{1,0:T(8,128)(2,1)} %param.8) | copy-start | bytes 393220
  2.9 16.3 %copy-start.1 = (bf16[128,4096]{1,0:T(8,128)(2,1)S(1)}, bf16[128,4096]{1,0:T(8,128)(2,1)}, u32[]{:S(2)}) copy-start(bf16[128,4096]{1,0:T(8,128)(2,1)} %param.9) | copy-start | bytes 3145732
  3.5 15.7 %copy-start.4 = (bf16[128,4096]{1,0:T(8,128)(2,1)S(1)}, bf16[128,4096]{1,0:T(8,128)(2,1)}, u32[]{:S(2)}) copy-start(bf16[128,4096]{1,0:T(8,128)(2,1)} %param.6) | copy-start | bytes 3145732
  4.2 9.6 %all-to-all-start.2 = ((f32[128,4,8]{0,2,1:T(8,128)}), f32[128,4,8]{0,2,1:T(8,128)S(1)}, u32[]{:S(2)}, u32[]{:S(2)}) async-start(f32[128,4,8]{0,2,1:T(8,128)} %bitcast.18), calls=%async_computation.2 | async-start | bytes 32768 | tf_op jit(solution)/shard_map/all_to_all | solution.py:153
  13.8 13.6 %all-to-all-start = ((bf16[128,4,384]{2,0,1:T(8,128)(2,1)}), bf16[128,4,384]{2,0,1:T(8,128)(2,1)}, u32[]{:S(2)}, u32[]{:S(2)}) async-start(bf16[128,4,384]{2,0,1:T(8,128)(2,1)} %pad_maximum_fusion.1), calls=%async_computation | async-start | bytes 786432 | tf_op jit(solution)/shard_map/all_to_all | solution.py:151
  27.4 49.0 %all-to-all-start.1 = ((bf16[128,4,2048]{2,0,1:T(8,128)(2,1)}), bf16[128,4,2048]{2,0,1:T(8,128)(2,1)S(1)}, u32[]{:S(2)}, u32[]{:S(2)}) async-start(bf16[128,4,2048]{2,0,1:T(8,128)(2,1)} %pad_maximum_fusion), calls=%async_computation.1 | async-start | bytes 4194304 | tf_op jit(solution)/shard_map/all_to_all | solution.py:163
  35.4 14.1 %collective-permute-start.3 = (bf16[512,384]{1,0:T(8,128)(2,1)}, bf16[512,384]{1,0:T(8,128)(2,1)S(1)}, u32[]{:S(2)}, u32[]{:S(2)}) collective-permute-start(bf16[512,384]{1,0:T(8,128)(2,1)} %bitcast.2), channel_id=1, source_target_pairs={{0,16},{4,20},{8,24},{12,28},{1,17},{5,21},{9,25},{13,29},{2,18},{... | collective-permute-start | bytes 1179656 | tf_op jit(solution)/shard_map/ppermute | solution.py:20
  36.7 14.8 %collective-permute-start.2 = (bf16[512,384]{1,0:T(8,128)(2,1)}, bf16[512,384]{1,0:T(8,128)(2,1)S(1)}, u32[]{:S(2)}, u32[]{:S(2)}) collective-permute-start(bf16[512,384]{1,0:T(8,128)(2,1)} %bitcast.2), channel_id=1, source_target_pairs={{0,12},{4,16},{8,20},{12,24},{16,28},{1,13},{5,17},{9,21},{13,25},... | collective-permute-start | bytes 1179656 | tf_op jit(solution)/shard_map/ppermute | solution.py:20
  39.6 17.5 %collective-permute-start.1 = (bf16[512,384]{1,0:T(8,128)(2,1)}, bf16[512,384]{1,0:T(8,128)(2,1)S(1)}, u32[]{:S(2)}, u32[]{:S(2)}) collective-permute-start(bf16[512,384]{1,0:T(8,128)(2,1)} %bitcast.2), channel_id=1, source_target_pairs={{0,8},{4,12},{8,16},{12,20},{16,24},{20,28},{1,9},{5,13},{9,17},{1... | collective-permute-start | bytes 1179656 | tf_op jit(solution)/shard_map/ppermute | solution.py:20
  40.9 18.1 %collective-permute-start = (bf16[512,384]{1,0:T(8,128)(2,1)}, bf16[512,384]{1,0:T(8,128)(2,1)S(1)}, u32[]{:S(2)}, u32[]{:S(2)}) collective-permute-start(bf16[512,384]{1,0:T(8,128)(2,1)} %bitcast.2), channel_id=1, source_target_pairs={{0,4},{4,8},{8,12},{12,16},{16,20},{20,24},{24,28},{1,5},{5,9},{9,... | collective-permute-start | bytes 1179656 | tf_op jit(solution)/shard_map/ppermute | solution.py:20
  59.0 0.7 copy-start.5
  154.5 1.7 copy-start.3
  156.4 7.0 %collective-permute-start.5 = (bf16[512,256]{1,0:T(8,128)(2,1)S(1)}, bf16[512,256]{1,0:T(8,128)(2,1)S(1)}, u32[]{:S(2)}, u32[]{:S(2)}) collective-permute-start(bf16[512,256]{1,0:T(8,128)(2,1)S(1)} %pad_maximum_fusion.3), channel_id=1, source_target_pairs={{8,0},{12,4},{16,8},{20,12},{24,16},{28,20},{9,1},{13,5},{17,9},{2... | collective-permute-start | bytes 786440 | tf_op jit(solution)/shard_map/ppermute | solution.py:20
  157.8 5.7 %collective-permute-start.6 = (bf16[512,256]{1,0:T(8,128)(2,1)S(1)}, bf16[512,256]{1,0:T(8,128)(2,1)S(1)}, u32[]{:S(2)}, u32[]{:S(2)}) collective-permute-start(bf16[512,256]{1,0:T(8,128)(2,1)S(1)} %pad_maximum_fusion.4), channel_id=1, source_target_pairs={{12,0},{16,4},{20,8},{24,12},{28,16},{13,1},{17,5},{21,9},{25,13},... | collective-permute-start | bytes 786440 | tf_op jit(solution)/shard_map/ppermute | solution.py:20
  159.1 6.6 %collective-permute-start.7 = (bf16[512,256]{1,0:T(8,128)(2,1)S(1)}, bf16[512,256]{1,0:T(8,128)(2,1)S(1)}, u32[]{:S(2)}, u32[]{:S(2)}) collective-permute-start(bf16[512,256]{1,0:T(8,128)(2,1)S(1)} %pad_maximum_fusion.5), channel_id=1, source_target_pairs={{16,0},{20,4},{24,8},{28,12},{17,1},{21,5},{25,9},{29,13},{18,2},{... | collective-permute-start | bytes 786440 | tf_op jit(solution)/shard_map/ppermute | solution.py:20
  160.5 16.7 %collective-permute-start.4 = (bf16[512,256]{1,0:T(8,128)(2,1)S(1)}, bf16[512,256]{1,0:T(8,128)(2,1)S(1)}, u32[]{:S(2)}, u32[]{:S(2)}) collective-permute-start(bf16[512,256]{1,0:T(8,128)(2,1)S(1)} %pad_maximum_fusion.2), channel_id=1, source_target_pairs={{4,0},{8,4},{12,8},{16,12},{20,16},{24,20},{28,24},{5,1},{9,5},{13... | collective-permute-start | bytes 786440 | tf_op jit(solution)/shard_map/ppermute | solution.py:20
  163.4 23.8 %copy-start.2 = (f32[512,1024]{1,0:T(8,128)S(1)}, f32[512,1024]{1,0:T(8,128)}, u32[]{:S(2)}) copy-start(f32[512,1024]{1,0:T(8,128)} %get-tuple-element.6) | copy-start | bytes 6291460
  178.1 17.5 %all-to-all-start.4 = ((bf16[4,128,1,256]{3,1,2,0:T(8,128)(2,1)}), bf16[4,128,1,256]{3,1,2,0:T(8,128)(2,1)S(1)}, u32[]{:S(2)}, u32[]{:S(2)}) async-start(bf16[4,128,1,256]{3,1,2,0:T(8,128)(2,1)} %bitcast.50), calls=%async_computation.4 | async-start | bytes 524288 | tf_op jit(solution)/shard_map/all_to_all | solution.py:207
  195.5 28.3 %all-to-all-start.3 = ((bf16[4,128,1,1024]{3,1,2,0:T(8,128)(2,1)}), bf16[4,128,1,1024]{3,1,2,0:T(8,128)(2,1)S(1)}, u32[]{:S(2)}, u32[]{:S(2)}) async-start(bf16[4,128,1,1024]{3,1,2,0:T(8,128)(2,1)} %bitcast.35), calls=%async_computation.3 | async-start | bytes 2097152 | tf_op jit(solution)/shard_map/all_to_all | solution.py:195

commit v2 on v1

--- a/solution.py
+++ b/solution.py
@@ -21,7 +21,7 @@
 
 
 def attn_kernel(flags_ref, q_ref, do_ref, rt_ref, qdoc_ref, kdoc_ref, k_ref, v_ref,
-                dq_ref, dk_ref, dv_ref, m_ref, l_ref, *, n_near, logit_scale):
+                dq_ref, dk_ref, dv_ref, bias_ref, m_ref, l_ref, *, n_near, logit_scale):
     head = pl.program_id(0)
     rows = q_ref.shape[0]
 
@@ -29,35 +29,35 @@
     def _():
         dk_ref[...] = jnp.zeros_like(dk_ref)
         dv_ref[...] = jnp.zeros_like(dv_ref)
+        key_id = lax.broadcasted_iota(jnp.int32, (rows, rows), 0)
+        query_id = lax.broadcasted_iota(jnp.int32, (rows, rows), 1)
+        qdoc = qdoc_ref[...]
+        for d in range(n_near):
+            @pl.when(flags_ref[d] > 0)
+            def _():
+                allowed = kdoc_ref[d] == qdoc
+                if d == 0:
+                    allowed = allowed & (key_id <= query_id)
+                bias_ref[d] = jnp.where(allowed, 0.0, masked_score)
 
     q = q_ref[...]
     do = do_ref[...]
-    qdoc = qdoc_ref[...]
-    row_id = lax.broadcasted_iota(jnp.int32, (rows, rows), 0)
-    col_id = lax.broadcasted_iota(jnp.int32, (rows, rows), 1)
-
-    def allowed_of(d):
-        same = qdoc == kdoc_ref[d]
-        if d == 0:
-            same = same & (col_id <= row_id)
-        return same
 
     def scores_of(d):
-        s = lax.dot_general(q, k_ref[d], (((1,), (1,)), ((), ())),
-                            preferred_element_type=jnp.float32) * logit_scale
-        return s
+        s = lax.dot_general(k_ref[d], q, (((1,), (1,)), ((), ())),
+                            preferred_element_type=jnp.float32)
+        return s * logit_scale + bias_ref[d]
 
     m_ref[...] = jnp.full(m_ref.shape, masked_score, jnp.float32)
     l_ref[...] = jnp.zeros(l_ref.shape, jnp.float32)
     for d in range(n_near):
         @pl.when(flags_ref[d] > 0)
         def _():
-            allowed = allowed_of(d)
-            s = jnp.where(allowed, scores_of(d), masked_score)
+            s = scores_of(d)
             m_old = m_ref[...]
-            m_new = jnp.maximum(m_old, jnp.max(s, axis=-1, keepdims=True))
+            m_new = jnp.maximum(m_old, jnp.max(s, axis=0, keepdims=True))
             l_ref[...] = l_ref[...] * jnp.exp(m_old - m_new) + jnp.sum(
-                jnp.where(allowed, jnp.exp(s - m_new), 0.0), axis=-1, keepdims=True)
+                jnp.exp(s - m_new), axis=0, keepdims=True)
             m_ref[...] = m_new
 
     log_total = m_ref[...] + jnp.log(l_ref[...])
@@ -66,18 +66,15 @@
     for d in range(n_near):
         @pl.when(flags_ref[d] > 0)
         def _():
-            allowed = allowed_of(d)
-            s = scores_of(d)
-            p = jnp.where(allowed, jnp.exp(s - log_total), 0.0)
-            dp = lax.dot_general(do, v_ref[d], (((1,), (1,)), ((), ())),
+            p = jnp.exp(scores_of(d) - log_total)
+            dp = lax.dot_general(v_ref[d], do, (((1,), (1,)), ((), ())),
                                  preferred_element_type=jnp.float32)
             ds = (p * (dp - rt)).astype(jnp.bfloat16)
             pb = p.astype(jnp.bfloat16)
-            dv_ref[d] += lax.dot_general(pb, do, (((0,), (0,)), ((), ())),
-                                         preferred_element_type=jnp.float32)
-            dk_ref[d] += lax.dot_general(ds, q, (((0,), (0,)), ((), ())),
-                                         preferred_element_type=jnp.float32)
-            dq_ref[...] += jnp.dot(ds, k_ref[d], preferred_element_type=jnp.float32)
+            dv_ref[d] += jnp.dot(pb, do, preferred_element_type=jnp.float32)
+            dk_ref[d] += jnp.dot(ds, q, preferred_element_type=jnp.float32)
+            dq_ref[...] += lax.dot_general(ds, k_ref[d], (((0,), (0,)), ((), ())),
+                                           preferred_element_type=jnp.float32)
 
 
 def block_attention(flags, q, do, rt, qdoc, kdoc, k, v):
@@ -100,9 +97,9 @@
             in_specs=[
                 pl.BlockSpec((rows, HEAD_WIDTH), lambda h, f: (0, h)),
                 pl.BlockSpec((rows, HEAD_WIDTH), lambda h, f: (0, h)),
-                pl.BlockSpec((1, rows, 1), lambda h, f: (h, 0, 0)),
-                pl.BlockSpec((rows, 1), lambda h, f: (0, 0)),
-                full3((n_near, 1, rows)),
+                pl.BlockSpec((1, 1, rows), lambda h, f: (h, 0, 0)),
+                pl.BlockSpec((1, rows), lambda h, f: (0, 0)),
+                full3((n_near, rows, 1)),
                 full3((n_near, rows, HEAD_WIDTH)),
                 full3((n_near, rows, HEAD_WIDTH)),
             ],
@@ -111,7 +108,11 @@
                 full3((n_near, rows, HEAD_WIDTH)),
                 full3((n_near, rows, HEAD_WIDTH)),
             ],
-            scratch_shapes=[pltpu.VMEM((rows, 1), jnp.float32), pltpu.VMEM((rows, 1), jnp.float32)],
+            scratch_shapes=[
+                pltpu.VMEM((n_near, rows, rows), jnp.float32),
+                pltpu.VMEM((1, rows), jnp.float32),
+                pltpu.VMEM((1, rows), jnp.float32),
+            ],
         ),
         compiler_params=pltpu.CompilerParams(dimension_semantics=("arbitrary",)),
         cost_estimate=pl.CostEstimate(flops=flops, transcendentals=2 * heads * n_near * rows * rows,
@@ -178,13 +179,13 @@
     flags = jnp.stack(flags)
     near_keys = jnp.stack([kvd[:, :kv_cols] for kvd in near_blocks])
     near_values = jnp.stack([kvd[:, kv_cols : 2 * kv_cols] for kvd in near_blocks])
-    near_docs = jnp.stack([kvd[:, 2 * kv_cols].astype(jnp.float32) for kvd in near_blocks])[:, None, :]
+    near_docs = jnp.stack([kvd[:, 2 * kv_cols].astype(jnp.float32) for kvd in near_blocks])[:, :, None]
     query_total, key_parts, value_parts = block_attention(
         flags,
         packed[:, :q_cols],
         packed[:, q_cols : 2 * q_cols],
-        row_terms_blk.transpose(1, 0)[:, :, None],
-        query_segment[:, None],
+        row_terms_blk.transpose(1, 0)[:, None, :],
+        query_segment[None, :],
         near_docs,
         near_keys,
         near_values,

time: 229 us -> 192 us (0.84); the launches traced: 226 us -> 194 us
  Pallas kernels: 76.7 us -> 51.5 us
  waiting for transfers between devices: 67.7 us -> 63.1 us
    pallas_call x1, Pallas kernels: 76.7 us -> 51.5 us  [block_attention(): pl.pallas_call(kern, out_shape=(jax.ShapeDtypeStruct((rows, cols), jnp.fl...]
    ppermute x8, waiting for transfers between devices: 21 us -> 15.2 us  [shifted(): return lax.ppermute(block, axis, route)]
    convert_element_type x0 -> x5, other arithmetic: none -> 2.39 us  [the longest x4 1.37 us: per_device(): kvd[:, 2 * kv_cols].astype(jnp.float32)]
  transfers between devices with their start and end apart: 13 -> 13, of which waited for: 9 -> 9; matrix products, arithmetic and copies ran while one was open for 10% -> 11% of each run, Pallas kernels for 0% -> 0%
where the time goes in v2:
time: 192 us; the launch traced here: 194 us
  waiting for transfers between devices  63.1 us (33%)
  Pallas kernels  51.5 us (27%)
  starting transfers between devices  42.8 us (22%)
  local copies, waits for them, and re-layouts  19.7 us (10%)
  other arithmetic  11.6 us (6%)
  between operations  5.79 us (3%)
    pallas_call x1, Pallas kernels, block_attention(): pl.pallas_call(kern, out_shape=(jax.ShapeDtypeStruct((rows, cols), jnp.fl...  51.5 us
    all_to_all x1, waiting for transfers between devices, per_device(): lax.all_to_all(query_grad, 'head', split_axis=0, concat_axis=2, tiled=True)  21.3 us
    ppermute x8, waiting for transfers between devices, shifted(): return lax.ppermute(block, axis, route)  15.2 us
    ppermute x8, starting transfers between devices, shifted(): return lax.ppermute(block, axis, route)  11.6 us
    all_to_all x1, waiting for transfers between devices, per_device(): lax.all_to_all(packed, 'head', split_axis=1, concat_axis=0, tiled=True)  9.86 us
    all_to_all x1, starting transfers between devices, per_device(): lax.all_to_all(out_packed, 'head', split_axis=0, concat_axis=2, tiled=True)  9.08 us
    unnamed x24, local copies, waits for them, and re-layouts  8.27 us
    all_to_all x1, waiting for transfers between devices, per_device(): lax.all_to_all(out_packed, 'head', split_axis=0, concat_axis=2, tiled=True)  7.16 us
  transfers between devices with their start and end apart: 13, of which 9 were waited for; matrix products, arithmetic and copies ran while one was open for 11% of the time, Pallas kernels for 0%

profile of v2, /device:TPU:14, one launch (start us, length us, event | category | flops | bytes accessed | tf_op | source)
XLA Modules:
  0.0 194.5 jit_solution(10799276513963452854)
XLA Ops:
  0.6 0.0 copy-start
  0.6 1.8 multiply_bitcast_fusion
  2.5 0.4 copy.49
  2.9 0.6 reduce_sum.9
  3.5 0.7 copy.36
  4.2 5.3 %all-to-all-start.2 = ((f32[128,4,8]{0,2,1:T(8,128)}), f32[128,4,8]{0,2,1:T(8,128)S(1)}, u32[]{:S(2)}, u32[]{:S(2)}) async-start(f32[128,4,8]{0,2,1:T(8,128)} %bitcast.18), calls=%async_computation.2 | async-start | bytes 32768 | tf_op jit(solution)/shard_map/all_to_all | solution.py:154
  9.6 0.1 broadcast_in_dim.6
  9.7 0.8 pad_maximum_fusion.1
  10.5 3.3 %all-to-all-done.2 = f32[128,4,8]{0,2,1:T(8,128)S(1)} async-done(((f32[128,4,8]{0,2,1:T(8,128)}), f32[128,4,8]{0,2,1:T(8,128)S(1)}, u32[]{:S(2)}, u32[]{:S(2)}) %all-to-all-start.2) | async-done | bytes 16416 | tf_op jit(solution)/shard_map/all_to_all | solution.py:154
  13.8 5.4 %all-to-all-start = ((bf16[128,4,384]{2,0,1:T(8,128)(2,1)}), bf16[128,4,384]{2,0,1:T(8,128)(2,1)}, u32[]{:S(2)}, u32[]{:S(2)}) async-start(bf16[128,4,384]{2,0,1:T(8,128)(2,1)} %pad_maximum_fusion.1), calls=%async_computation | async-start | bytes 786432 | tf_op jit(solution)/shard_map/all_to_all | solution.py:152
  19.2 0.2 copy_bitcast_fusion
  19.4 1.5 pad_maximum_fusion
  21.0 6.4 %all-to-all-done = bf16[128,4,384]{2,0,1:T(8,128)(2,1)} async-done(((bf16[128,4,384]{2,0,1:T(8,128)(2,1)}), bf16[128,4,384]{2,0,1:T(8,128)(2,1)}, u32[]{:S(2)}, u32[]{:S(2)}) %all-to-all-start) | async-done | bytes 393248 | tf_op jit(solution)/shard_map/all_to_all | solution.py:152
  27.4 6.1 %all-to-all-start.1 = ((bf16[128,4,2048]{2,0,1:T(8,128)(2,1)}), bf16[128,4,2048]{2,0,1:T(8,128)(2,1)S(1)}, u32[]{:S(2)}, u32[]{:S(2)}) async-start(bf16[128,4,2048]{2,0,1:T(8,128)(2,1)} %pad_maximum_fusion), calls=%async_computation.1 | async-start | bytes 4194304 | tf_op jit(solution)/shard_map/all_to_all | solution.py:164
  33.4 1.3 collective-permute-start.3
  34.7 1.3 collective-permute-start.2
  36.0 1.3 collective-permute-start.1
  37.3 1.9 collective-permute-start
  39.3 0.6 broadcast_in_dim.14.rt_ref
  39.9 1.2 slice.161
  41.0 1.0 convert_reduce_fusion.4
  42.1 1.7 fusion.8
  43.8 3.8 %collective-permute-done.3 = bf16[512,384]{1,0:T(8,128)(2,1)S(1)} collective-permute-done((bf16[512,384]{1,0:T(8,128)(2,1)}, bf16[512,384]{1,0:T(8,128)(2,1)S(1)}, u32[]{:S(2)}, u32[]{:S(2)}) %collective-permute-start.3) | collective-permute-done | bytes 393248 | tf_op jit(solution)/shard_map/ppermute | solution.py:20
  47.6 0.5 slice.164
  49.3 0.5 slice.163
  51.0 3.8 %collective-permute-done.1 = bf16[512,384]{1,0:T(8,128)(2,1)S(1)} collective-permute-done((bf16[512,384]{1,0:T(8,128)(2,1)}, bf16[512,384]{1,0:T(8,128)(2,1)S(1)}, u32[]{:S(2)}, u32[]{:S(2)}) %collective-permute-start.1) | collective-permute-done | bytes 393248 | tf_op jit(solution)/shard_map/ppermute | solution.py:20
  54.8 0.5 slice.162
  56.6 1.2 slice.160
  59.0 0.1 stack.69
  59.1 0.6 stack.70.flags_ref
  59.6 0.1 convert_reduce_fusion
  59.8 0.1 convert_reduce_fusion.1
  59.9 0.1 convert_reduce_fusion.2
  60.0 1.0 convert_reduce_fusion.3
  61.1 1.5 copy.37.kdoc_ref
  62.6 1.7 fusion.7
  64.3 0.7 fusion.6
  65.0 0.7 fusion.5
  65.7 0.7 fusion.4
  66.5 9.9 %all-to-all-done.1 = bf16[128,4,2048]{2,0,1:T(8,128)(2,1)S(1)} async-done(((bf16[128,4,2048]{2,0,1:T(8,128)(2,1)}), bf16[128,4,2048]{2,0,1:T(8,128)(2,1)S(1)}, u32[]{:S(2)}, u32[]{:S(2)}) %all-to-all-start.1) | async-done | bytes 2097184 | tf_op jit(solution)/shard_map/all_to_all | solution.py:164
  76.3 1.5 fusion.14
  77.9 51.5 %shard_map.85 = (f32[512,1024]{1,0:T(8,128)}, f32[5,512,128]{2,1,0:T(8,128)}, f32[5,512,128]{2,1,0:T(8,128)}) custom-call(s32[5]{0:T(128)} %stack.70.flags_ref, bf16[512,1024]{1,0:T(8,128)(2,1)} %get-tuple-element.13.q_ref, bf16[512,1024]{1,0:T(8,128)(2,1)} %get-tuple-element.12.do_ref, f32[8,1,512]{2,1,0:T(1,128)} %broadcast_in_dim.14.rt_ref, ...), custom_call_target="tpu_custom_call" | custom-call | flops 16106127360 | bytes 9437184 | tf_op jit(solution)/shard_map/pallas_call | solution.py:87
  129.4 1.5 convert.43
  130.9 0.2 copy-done.3
  131.1 0.1 convert.44
  131.2 1.3 collective-permute-start.5
  132.6 1.3 collective-permute-start.6
  133.9 1.3 collective-permute-start.7
  135.3 1.9 collective-permute-start.4
  137.2 1.0 slice_bitcast_fusion.1
  138.3 2.3 %collective-permute-done.7 = bf16[512,256]{1,0:T(8,128)(2,1)S(1)} collective-permute-done((bf16[512,256]{1,0:T(8,128)(2,1)S(1)}, bf16[512,256]{1,0:T(8,128)(2,1)S(1)}, u32[]{:S(2)}, u32[]{:S(2)}) %collective-permute-start.7) | collective-permute-done | bytes 262176 | tf_op jit(solution)/shard_map/ppermute | solution.py:20
  140.6 5.2 %collective-permute-done.4 = bf16[512,256]{1,0:T(8,128)(2,1)S(1)} collective-permute-done((bf16[512,256]{1,0:T(8,128)(2,1)S(1)}, bf16[512,256]{1,0:T(8,128)(2,1)S(1)}, u32[]{:S(2)}, u32[]{:S(2)}) %collective-permute-start.4) | collective-permute-done | bytes 262176 | tf_op jit(solution)/shard_map/ppermute | solution.py:20
  145.8 0.1 fusion.2
  146.0 0.7 pad_maximum_fusion.6
  146.7 9.1 %all-to-all-start.4 = ((bf16[4,128,1,256]{3,1,2,0:T(8,128)(2,1)}), bf16[4,128,1,256]{3,1,2,0:T(8,128)(2,1)S(1)}, u32[]{:S(2)}, u32[]{:S(2)}) async-start(bf16[4,128,1,256]{3,1,2,0:T(8,128)(2,1)} %bitcast.50), calls=%async_computation.4 | async-start | bytes 524288 | tf_op jit(solution)/shard_map/all_to_all | solution.py:208
  155.8 1.2 multiply_convert_fusion
  157.0 7.2 %all-to-all-done.4 = bf16[4,128,1,256]{3,1,2,0:T(8,128)(2,1)S(1)} async-done(((bf16[4,128,1,256]{3,1,2,0:T(8,128)(2,1)}), bf16[4,128,1,256]{3,1,2,0:T(8,128)(2,1)S(1)}, u32[]{:S(2)}, u32[]{:S(2)}) %all-to-all-start.4) | async-done | bytes 262176 | tf_op jit(solution)/shard_map/all_to_all | solution.py:208
  164.2 5.3 %all-to-all-start.3 = ((bf16[4,128,1,1024]{3,1,2,0:T(8,128)(2,1)}), bf16[4,128,1,1024]{3,1,2,0:T(8,128)(2,1)S(1)}, u32[]{:S(2)}, u32[]{:S(2)}) async-start(bf16[4,128,1,1024]{3,1,2,0:T(8,128)(2,1)} %bitcast.35), calls=%async_computation.3 | async-start | bytes 2097152 | tf_op jit(solution)/shard_map/all_to_all | solution.py:196
  169.5 0.2 copy.41
  169.7 0.8 copy.44
  170.5 0.8 copy.43
  171.2 21.3 %all-to-all-done.3 = bf16[4,128,1,1024]{3,1,2,0:T(8,128)(2,1)S(1)} async-done(((bf16[4,128,1,1024]{3,1,2,0:T(8,128)(2,1)}), bf16[4,128,1,1024]{3,1,2,0:T(8,128)(2,1)S(1)}, u32[]{:S(2)}, u32[]{:S(2)}) %all-to-all-start.3) | async-done | bytes 1048608 | tf_op jit(solution)/shard_map/all_to_all | solution.py:196
  192.5 0.7 copy.39
  193.2 1.3 copy.42
  (31 shorter events, 0.5 us)
Async XLA Ops:
  0.6 8.9 %copy-start = (bf16[128,512]{1,0:T(8,128)(2,1)S(1)}, bf16[128,512]{1,0:T(8,128)(2,1)}, u32[]{:S(2)}) copy-start(bf16[128,512]{1,0:T(8,128)(2,1)} %param.7) | copy-start | bytes 393220
  2.9 6.7 %copy-start.7 = (s32[128]{0:T(128)S(1)}, s32[128]{0:T(128)}, u32[]{:S(2)}) copy-start(s32[128]{0:T(128)} %param.11) | copy-start | bytes 1540
  2.9 6.7 %copy-start.5 = (bf16[128,512]{1,0:T(8,128)(2,1)S(1)}, bf16[128,512]{1,0:T(8,128)(2,1)}, u32[]{:S(2)}) copy-start(bf16[128,512]{1,0:T(8,128)(2,1)} %param.8) | copy-start | bytes 393220
  2.9 16.3 %copy-start.1 = (bf16[128,4096]{1,0:T(8,128)(2,1)S(1)}, bf16[128,4096]{1,0:T(8,128)(2,1)}, u32[]{:S(2)}) copy-start(bf16[128,4096]{1,0:T(8,128)(2,1)} %param.9) | copy-start | bytes 3145732
  3.5 15.7 %copy-start.4 = (bf16[128,4096]{1,0:T(8,128)(2,1)S(1)}, bf16[128,4096]{1,0:T(8,128)(2,1)}, u32[]{:S(2)}) copy-start(bf16[128,4096]{1,0:T(8,128)(2,1)} %param.6) | copy-start | bytes 3145732
  4.2 9.6 %all-to-all-start.2 = ((f32[128,4,8]{0,2,1:T(8,128)}), f32[128,4,8]{0,2,1:T(8,128)S(1)}, u32[]{:S(2)}, u32[]{:S(2)}) async-start(f32[128,4,8]{0,2,1:T(8,128)} %bitcast.18), calls=%async_computation.2 | async-start | bytes 32768 | tf_op jit(solution)/shard_map/all_to_all | solution.py:154
  13.8 13.6 %all-to-all-start = ((bf16[128,4,384]{2,0,1:T(8,128)(2,1)}), bf16[128,4,384]{2,0,1:T(8,128)(2,1)}, u32[]{:S(2)}, u32[]{:S(2)}) async-start(bf16[128,4,384]{2,0,1:T(8,128)(2,1)} %pad_maximum_fusion.1), calls=%async_computation | async-start | bytes 786432 | tf_op jit(solution)/shard_map/all_to_all | solution.py:152
  27.4 49.0 %all-to-all-start.1 = ((bf16[128,4,2048]{2,0,1:T(8,128)(2,1)}), bf16[128,4,2048]{2,0,1:T(8,128)(2,1)S(1)}, u32[]{:S(2)}, u32[]{:S(2)}) async-start(bf16[128,4,2048]{2,0,1:T(8,128)(2,1)} %pad_maximum_fusion), calls=%async_computation.1 | async-start | bytes 4194304 | tf_op jit(solution)/shard_map/all_to_all | solution.py:164
  33.4 14.1 %collective-permute-start.3 = (bf16[512,384]{1,0:T(8,128)(2,1)}, bf16[512,384]{1,0:T(8,128)(2,1)S(1)}, u32[]{:S(2)}, u32[]{:S(2)}) collective-permute-start(bf16[512,384]{1,0:T(8,128)(2,1)} %bitcast.2), channel_id=1, source_target_pairs={{0,16},{4,20},{8,24},{12,28},{1,17},{5,21},{9,25},{13,29},{2,18},{... | collective-permute-start | bytes 1179656 | tf_op jit(solution)/shard_map/ppermute | solution.py:20
  34.7 14.6 %collective-permute-start.2 = (bf16[512,384]{1,0:T(8,128)(2,1)}, bf16[512,384]{1,0:T(8,128)(2,1)S(1)}, u32[]{:S(2)}, u32[]{:S(2)}) collective-permute-start(bf16[512,384]{1,0:T(8,128)(2,1)} %bitcast.2), channel_id=1, source_target_pairs={{0,12},{4,16},{8,20},{12,24},{16,28},{1,13},{5,17},{9,21},{13,25},... | collective-permute-start | bytes 1179656 | tf_op jit(solution)/shard_map/ppermute | solution.py:20
  36.0 18.8 %collective-permute-start.1 = (bf16[512,384]{1,0:T(8,128)(2,1)}, bf16[512,384]{1,0:T(8,128)(2,1)S(1)}, u32[]{:S(2)}, u32[]{:S(2)}) collective-permute-start(bf16[512,384]{1,0:T(8,128)(2,1)} %bitcast.2), channel_id=1, source_target_pairs={{0,8},{4,12},{8,16},{12,20},{16,24},{20,28},{1,9},{5,13},{9,17},{1... | collective-permute-start | bytes 1179656 | tf_op jit(solution)/shard_map/ppermute | solution.py:20
  37.3 19.2 %collective-permute-start = (bf16[512,384]{1,0:T(8,128)(2,1)}, bf16[512,384]{1,0:T(8,128)(2,1)}, u32[]{:S(2)}, u32[]{:S(2)}) collective-permute-start(bf16[512,384]{1,0:T(8,128)(2,1)} %bitcast.2), channel_id=1, source_target_pairs={{0,4},{4,8},{8,12},{12,16},{16,20},{20,24},{24,28},{1,5},{5,9},{9,... | collective-permute-start | bytes 1179656 | tf_op jit(solution)/shard_map/ppermute | solution.py:20
  42.1 24.4 %copy-start.6 = (f32[512]{0:T(512)}, f32[512]{0:T(512)S(1)}, u32[]{:S(2)}) copy-start(f32[512]{0:T(512)S(1)} %convert_reduce_fusion.4) | copy-start | bytes 6148
  129.3 1.7 copy-start.3
  131.2 7.0 %collective-permute-start.5 = (bf16[512,256]{1,0:T(8,128)(2,1)S(1)}, bf16[512,256]{1,0:T(8,128)(2,1)S(1)}, u32[]{:S(2)}, u32[]{:S(2)}) collective-permute-start(bf16[512,256]{1,0:T(8,128)(2,1)S(1)} %pad_maximum_fusion.3), channel_id=1, source_target_pairs={{8,0},{12,4},{16,8},{20,12},{24,16},{28,20},{9,1},{13,5},{17,9},{2... | collective-permute-start | bytes 786440 | tf_op jit(solution)/shard_map/ppermute | solution.py:20
  132.6 5.7 %collective-permute-start.6 = (bf16[512,256]{1,0:T(8,128)(2,1)S(1)}, bf16[512,256]{1,0:T(8,128)(2,1)S(1)}, u32[]{:S(2)}, u32[]{:S(2)}) collective-permute-start(bf16[512,256]{1,0:T(8,128)(2,1)S(1)} %pad_maximum_fusion.4), channel_id=1, source_target_pairs={{12,0},{16,4},{20,8},{24,12},{28,16},{13,1},{17,5},{21,9},{25,13},... | collective-permute-start | bytes 786440 | tf_op jit(solution)/shard_map/ppermute | solution.py:20
  133.9 6.6 %collective-permute-start.7 = (bf16[512,256]{1,0:T(8,128)(2,1)S(1)}, bf16[512,256]{1,0:T(8,128)(2,1)S(1)}, u32[]{:S(2)}, u32[]{:S(2)}) collective-permute-start(bf16[512,256]{1,0:T(8,128)(2,1)S(1)} %pad_maximum_fusion.5), channel_id=1, source_target_pairs={{16,0},{20,4},{24,8},{28,12},{17,1},{21,5},{25,9},{29,13},{18,2},{... | collective-permute-start | bytes 786440 | tf_op jit(solution)/shard_map/ppermute | solution.py:20
  135.3 10.5 %collective-permute-start.4 = (bf16[512,256]{1,0:T(8,128)(2,1)S(1)}, bf16[512,256]{1,0:T(8,128)(2,1)S(1)}, u32[]{:S(2)}, u32[]{:S(2)}) collective-permute-start(bf16[512,256]{1,0:T(8,128)(2,1)S(1)} %pad_maximum_fusion.2), channel_id=1, source_target_pairs={{4,0},{8,4},{12,8},{16,12},{20,16},{24,20},{28,24},{5,1},{9,5},{13... | collective-permute-start | bytes 786440 | tf_op jit(solution)/shard_map/ppermute | solution.py:20
  138.2 17.6 %copy-start.2 = (f32[512,1024]{1,0:T(8,128)S(1)}, f32[512,1024]{1,0:T(8,128)}, u32[]{:S(2)}) copy-start(f32[512,1024]{1,0:T(8,128)} %get-tuple-element.6) | copy-start | bytes 6291460
  146.7 17.5 %all-to-all-start.4 = ((bf16[4,128,1,256]{3,1,2,0:T(8,128)(2,1)}), bf16[4,128,1,256]{3,1,2,0:T(8,128)(2,1)S(1)}, u32[]{:S(2)}, u32[]{:S(2)}) async-start(bf16[4,128,1,256]{3,1,2,0:T(8,128)(2,1)} %bitcast.50), calls=%async_computation.4 | async-start | bytes 524288 | tf_op jit(solution)/shard_map/all_to_all | solution.py:208
  164.2 28.3 %all-to-all-start.3 = ((bf16[4,128,1,1024]{3,1,2,0:T(8,128)(2,1)}), bf16[4,128,1,1024]{3,1,2,0:T(8,128)(2,1)S(1)}, u32[]{:S(2)}, u32[]{:S(2)}) async-start(bf16[4,128,1,1024]{3,1,2,0:T(8,128)(2,1)} %bitcast.35), calls=%async_computation.3 | async-start | bytes 2097152 | tf_op jit(solution)/shard_map/all_to_all | solution.py:196
